TPU v7x, 32 devices: a whole 2x2x4 slice. The times are simulated.
32 devices in a mesh: ctx: 8 (over z, y), grp: 4 (over x, core).
Axes of the slice: x: 2, y: 2, z: 4, core: 2. Of those that a mesh axis runs over, the one named last changes fastest.
Arguments:
- query: bfloat16 [1024, 12288], P('ctx', 'grp')
- land_keys: bfloat16 [32, 768], P('ctx')
- land_values: bfloat16 [32, 512], P('ctx'), may hold values from -6 to 6
- d_out: bfloat16 [1024, 8192], P('ctx', 'grp'), may hold values from -6 to 6
- doc_start: int32 [1024], P('ctx'), may hold values from 0 to 1023, as said below
Outputs:
- branch_out: bfloat16 [1024, 8192], P('ctx', 'grp')
- d_query: float32 [1024, 12288], P('ctx', 'grp')
- d_keys: float32 [32, 768], P('ctx')
- d_values: float32 [32, 512], P('ctx')
Inputs may be any that keep to these rules, and one draw needn't show every extreme that they name: doc_start never decreases from one position to the next, doc_start[t] <= t, a document starts at position 0, and one starts at the last position.
All inputs are finite; a program needn't handle non-finite values.
Results may differ from a plain program's by a relative error of at most 0.0049.
Values may be sent and summed in bfloat16 or wider, within the bound.
No kernel may reach another device: no remote copies, remote signals or barrier semaphores. Data moves between devices by JAX's collectives and lax.ppermute only.
A program may use at most 64 MiB of HBM per device.

v0:
```python
import math
import jax
import jax.numpy as jnp
from jax import lax
from jax.sharding import PartitionSpec as P

KVG = 4
DK = 192
DV = 128
BLK = 32


def shards(query, land_keys, land_values, d_out, doc_start):
    tok_rows = query.shape[0]
    head_count = query.shape[1] // DK
    nl_local = land_keys.shape[0]
    score_scale = 1.0 / math.sqrt(DK)
    group_id = lax.axis_index("grp") // (lax.axis_size("grp") // KVG)
    group_keys = lax.dynamic_slice_in_dim(land_keys, group_id * DK, DK, 1)
    group_values = lax.dynamic_slice_in_dim(land_values, group_id * DV, DV, 1)
    queries = query.reshape(tok_rows, head_count, DK)
    grads_in = d_out.reshape(tok_rows, head_count, DV)
    ctx_index = lax.axis_index("ctx")
    positions = ctx_index * tok_rows + jnp.arange(tok_rows, dtype=jnp.int32)
    keys_whole, values_whole = (
        lax.all_gather(group_keys, "ctx", axis=0, tiled=True),
        lax.all_gather(group_values, "ctx", axis=0, tiled=True),
    )
    columns = jnp.arange(keys_whole.shape[0], dtype=jnp.int32)
    allowed = (columns[None, :] * BLK >= doc_start[:, None]) & (
        (columns[None, :] + 1) * BLK <= positions[:, None] + 1
    )
    scores = (
        jnp.einsum("thd,jd->thj", queries, keys_whole, preferred_element_type=jnp.float32)
        * score_scale
    )
    masked, allowed = (jnp.where(allowed[:, None, :], scores, -1e30), allowed[:, None, :])
    peak = jnp.maximum(jnp.max(masked, axis=2), 0.0)
    expo = jnp.where(allowed, jnp.exp(masked - peak[..., None]), 0.0)
    denom = jnp.exp(-peak) + jnp.sum(expo, axis=2)
    weight = expo / denom[..., None]
    weight_b = weight.astype(jnp.bfloat16)
    context = jnp.einsum("thj,je->the", weight_b, values_whole, preferred_element_type=jnp.float32)
    branch_out = context.astype(jnp.bfloat16).reshape(tok_rows, head_count * DV)
    delta = jnp.sum(grads_in.astype(jnp.float32) * context, axis=2)
    d_weight = jnp.einsum("the,je->thj", grads_in, values_whole, preferred_element_type=jnp.float32)
    d_score_b = (weight * (d_weight - delta[..., None])).astype(jnp.bfloat16)
    d_query = (
        jnp.einsum("thj,jd->thd", d_score_b, keys_whole, preferred_element_type=jnp.float32)
        * score_scale
    ).reshape(tok_rows, head_count * DK)
    key_grad = (
        jnp.einsum("thj,thd->jd", d_score_b, queries, preferred_element_type=jnp.float32)
        * score_scale
    )
    value_grad = jnp.einsum("thj,the->je", weight_b, grads_in, preferred_element_type=jnp.float32)
    owned = lax.psum_scatter(
        jnp.concatenate([key_grad, value_grad], axis=1), "ctx", scatter_dimension=0, tiled=True
    )
    slots = (jnp.arange(KVG, dtype=jnp.int32) == group_id).astype(jnp.float32)
    placed = owned[:, None, :] * slots[None, :, None]
    totals = lax.psum(placed, "grp")
    d_keys = totals[:, :, :DK].reshape(nl_local, KVG * DK)
    d_values = totals[:, :, DK:].reshape(nl_local, KVG * DV)
    return (branch_out, d_query, d_keys, d_values)


def solution(mesh):
    return jax.shard_map(
        shards,
        mesh=mesh,
        in_specs=(P("ctx", "grp"), P("ctx", None), P("ctx", None), P("ctx", "grp"), P("ctx")),
        out_specs=(P("ctx", "grp"), P("ctx", "grp"), P("ctx", None), P("ctx", None)),
        check_vma=False,
    )
```

profile of v0, /device:TPU:0, one launch (start us, length us, event | category | flops | bytes accessed | tf_op | source)
XLA Modules:
  0.0 104.1 jit_solution(3525271043548078328)
XLA Ops:
  0.6 0.0 copy-start
  0.6 0.0 copy-start.1
  0.7 1.3 %dynamic-slice = u32[1]{0:T(128)} dynamic-slice(u32[32]{0:T(128)} %constant.50, u32[]{:T(128)S(6)} %add.60), dynamic_slice_sizes={1} | dynamic-slice | bytes 12
  2.7 0.7 dynamic-slice_bitcast_fusion.1
  3.3 0.0 copy-done
  3.3 0.1 dynamic-slice_bitcast_fusion
  3.4 0.7 compare_and_fusion
  4.2 22.3 %all-gather.1 = bf16[8,4,128]{2,1,0:T(4,128)(2,1)S(1)} all-gather(bf16[1,4,128]{2,1,0:T(4,128)(2,1)S(1)} %dynamic-slice_bitcast_fusion.1), channel_id=1, replica_groups=mesh['ctx'=8,'grp'=4] {'ctx'}, dimensions={0}, use_global_device_ids=true | all-gather | bytes 9216 | tf_op jit(solution)/shard_map/all_gather | solution.py:27
  26.5 26.1 %all-gather = bf16[8,4,192]{2,1,0:T(4,128)(2,1)S(1)} all-gather(bf16[1,4,192]{2,1,0:T(4,128)(2,1)S(1)} %dynamic-slice_bitcast_fusion), channel_id=1, replica_groups=mesh['ctx'=8,'grp'=4] {'ctx'}, dimensions={0}, use_global_device_ids=true | all-gather | bytes 13824 | tf_op jit(solution)/shard_map/all_gather | solution.py:26
  52.6 1.3 %copy.23 = bf16[128,2048]{0,1:T(8,128)(2,1)S(1)} copy(bf16[128,2048]{1,0:T(8,128)(2,1)} %param.8) | data formatting | bytes 1048576 | tf_op args[3]
  53.9 0.0 copy-done.1
  53.9 0.4 copy.22
  54.3 0.3 fusion.13
  54.6 0.1 fusion.7
  54.7 0.3 convolution_bitcast_fusion.1
  55.0 0.4 multiply_reduce_fusion
  55.3 0.2 fusion.4
  55.6 0.3 fusion.5
  55.9 0.1 pad_maximum_fusion
  56.0 33.4 %all-reduce = f32[32,320]{1,0:T(8,128)S(1)} all-reduce(f32[32,320]{1,0:T(8,128)S(1)} %pad_maximum_fusion), channel_id=2, replica_groups=mesh['ctx'=8,'grp'=4] {'ctx'}, use_global_device_ids=true, to_apply=%region_3.4.clone | all-reduce | flops 10240 | bytes 81920
  89.4 1.0 copy.26
  90.4 0.1 broadcast_multiply_fusion
  90.5 10.3 %psum.7 = f32[4,4,320]{2,1,0:T(4,128)S(1)} all-reduce(f32[4,4,320]{2,1,0:T(4,128)S(1)} %broadcast_multiply_fusion), channel_id=1, replica_groups=mesh['ctx'=8,'grp'=4] {'grp'}, use_global_device_ids=true, to_apply=%region_4.5 | all-reduce | flops 5120 | bytes 40960 | tf_op jit(solution)/shard_map/psum | solution.py:62
  100.7 0.1 slice_bitcast_fusion
  100.8 0.7 reshape.112
  101.5 0.6 copy.32
  102.1 0.4 convolution_multiply_fusion
  102.5 1.6 %copy.27 = f32[128,3072]{1,0:T(8,128)} copy(f32[128,3072]{0,1:T(8,128)S(1)} %bitcast.46) | data formatting | bytes 3145728
  (8 shorter events, 0.1 us)
Async XLA Ops:
  0.6 2.7 %copy-start = (bf16[4,768]{1,0:T(4,128)(2,1)S(1)}, bf16[4,768]{1,0:T(4,128)(2,1)}, u32[]{:S(2)}) copy-start(bf16[4,768]{1,0:T(4,128)(2,1)} %param.6) | copy-start | bytes 18436
  0.6 53.3 %copy-start.1 = (bf16[128,3072]{1,0:T(8,128)(2,1)S(1)}, bf16[128,3072]{1,0:T(8,128)(2,1)}, u32[]{:S(2)}) copy-start(bf16[128,3072]{1,0:T(8,128)(2,1)} %param.5) | copy-start | bytes 2359300
where the time goes:
time: 104 us
  blocking collectives  92 us (88%)
  local copies, waits for them, and re-layouts  7.81 us (8%)
  matrix products  1.87 us (2%)
  between operations  1.44 us (1%)
    unnamed x1, blocking collectives  33.4 us
    all_gather x1, blocking collectives, shards(): lax.all_gather(group_keys, 'ctx', axis=0, tiled=True)  26.1 us
    all_gather x1, blocking collectives, shards(): lax.all_gather(group_values, 'ctx', axis=0, tiled=True)  22.3 us
    psum x1, blocking collectives, shards(): totals = lax.psum(placed, 'grp')  10.3 us
    unnamed x15, local copies, waits for them, and re-layouts  7.12 us

commit v1 on v0

--- a/solution.py
+++ b/solution.py
@@ -3,6 +3,7 @@
 import jax.numpy as jnp
 from jax import lax
 from jax.sharding import PartitionSpec as P
+from jax.lax import axis_size, ppermute
 
 KVG = 4
 DK = 192
@@ -59,7 +60,17 @@
     )
     slots = (jnp.arange(KVG, dtype=jnp.int32) == group_id).astype(jnp.float32)
     placed = owned[:, None, :] * slots[None, :, None]
-    totals = lax.psum(placed, "grp")
+
+    def group_sections(base_x):
+        which_axis = "grp"
+        n_slots = axis_size(which_axis)
+        clean = base_x
+        local_part = lambda b_now: [(rr, rr ^ b_now) for rr in range(n_slots)]
+        for jj in range(n_slots.bit_length() - 1):
+            clean = clean + ppermute(clean, axis_name=which_axis, perm=local_part(1 << jj))
+        return clean
+
+    totals = group_sections(placed)
     d_keys = totals[:, :, :DK].reshape(nl_local, KVG * DK)
     d_values = totals[:, :, DK:].reshape(nl_local, KVG * DV)
     return (branch_out, d_query, d_keys, d_values)

time: 104 us -> 95.7 us (0.920)
  blocking collectives: 92 us -> 81.8 us
  starting transfers between devices: 0 us -> 1.52 us
  waiting for transfers between devices: 0 us -> 1.18 us
    psum x1 -> x0, blocking collectives: 10.3 us -> none  [shards(): totals = lax.psum(placed, 'grp')]
    ppermute x0 -> x2, starting transfers between devices: none -> 1.52 us  [group_sections(): ppermute(clean, axis_name=which_axis, perm=local_part(1 << jj))]
    ppermute x0 -> x2, waiting for transfers between devices: none -> 1.18 us  [group_sections(): ppermute(clean, axis_name=which_axis, perm=local_part(1 << jj))]
    unnamed x15 -> x19, local copies, waits for them, and re-layouts: 7.12 us -> 6.46 us
  transfers between devices with their start and end apart: 0 -> 2, of which waited for: 0 -> 1; matrix products, arithmetic and copies ran while one was open for 0% -> 3% of each run, Pallas kernels for 0% -> 0%
where the time goes in v1:
time: 95.7 us; the launch traced here: 95.5 us
  blocking collectives  81.8 us (85%)
  local copies, waits for them, and re-layouts  7.15 us (7%)
  matrix products  1.86 us (2%)
  starting transfers between devices  1.52 us (2%)
  between operations  1.51 us (2%)
  waiting for transfers between devices  1.18 us (1%)
    unnamed x1, blocking collectives  33.4 us
    all_gather x1, blocking collectives, shards(): lax.all_gather(group_keys, 'ctx', axis=0, tiled=True)  26.1 us
    all_gather x1, blocking collectives, shards(): lax.all_gather(group_values, 'ctx', axis=0, tiled=True)  22.3 us
    unnamed x19, local copies, waits for them, and re-layouts  6.46 us
  transfers between devices with their start and end apart: 2, of which 1 were waited for; matrix products, arithmetic and copies ran while one was open for 3% of the time, Pallas kernels for 0%

profile of v1, /device:TPU:0, one launch (start us, length us, event | category | flops | bytes accessed | tf_op | source)
XLA Modules:
  0.0 95.5 jit_solution(7740602941243683399)
XLA Ops:
  0.6 0.0 copy-start
  0.6 0.0 copy-start.1
  0.7 0.0 copy-start.2
  0.7 0.7 dynamic-slice_bitcast_fusion.1
  1.5 22.3 %all-gather.1 = bf16[8,4,128]{2,1,0:T(4,128)(2,1)S(1)} all-gather(bf16[1,4,128]{2,1,0:T(4,128)(2,1)S(1)} %dynamic-slice_bitcast_fusion.1), channel_id=1, replica_groups=mesh['ctx'=8,'grp'=4] {'ctx'}, dimensions={0}, use_global_device_ids=true | all-gather | bytes 9216 | tf_op jit(solution)/shard_map/all_gather | solution.py:28
  23.8 0.0 copy-done
  23.8 0.1 dynamic-slice_bitcast_fusion
  23.9 26.1 %all-gather = bf16[8,4,192]{2,1,0:T(4,128)(2,1)S(1)} all-gather(bf16[1,4,192]{2,1,0:T(4,128)(2,1)S(1)} %dynamic-slice_bitcast_fusion), channel_id=1, replica_groups=mesh['ctx'=8,'grp'=4] {'ctx'}, dimensions={0}, use_global_device_ids=true | all-gather | bytes 13824 | tf_op jit(solution)/shard_map/all_gather | solution.py:27
  50.0 1.3 %copy.23 = bf16[128,2048]{0,1:T(8,128)(2,1)S(1)} copy(bf16[128,2048]{1,0:T(8,128)(2,1)} %param.8) | data formatting | bytes 1048576 | tf_op args[3]
  51.3 0.0 copy-done.1
  51.3 0.4 copy.22
  51.7 0.0 copy-done.2
  51.7 0.1 compare_and_fusion
  51.8 0.3 fusion.14
  52.1 0.1 fusion.7
  52.2 0.3 convolution_bitcast_fusion.1
  52.4 0.4 multiply_reduce_fusion
  52.8 0.0 copy-start.3
  52.8 0.2 fusion.4
  53.0 0.3 fusion.5
  53.4 0.1 pad_maximum_fusion
  53.5 33.4 %all-reduce = f32[32,320]{1,0:T(8,128)S(1)} all-reduce(f32[32,320]{1,0:T(8,128)S(1)} %pad_maximum_fusion), channel_id=2, replica_groups=mesh['ctx'=8,'grp'=4] {'ctx'}, use_global_device_ids=true, to_apply=%region_3.4.clone | all-reduce | flops 10240 | bytes 81920
  86.9 0.0 copy-done.3
  86.9 0.6 dynamic-slice
  88.1 0.1 broadcast_multiply_fusion
  88.2 0.0 collective-permute-start
  88.2 1.2 %collective-permute-done = f32[4,4,320]{2,1,0:T(4,128)S(1)} collective-permute-done((f32[4,4,320]{2,1,0:T(4,128)S(1)}, f32[4,4,320]{2,1,0:T(4,128)S(1)}, u32[]{:S(2)}, u32[]{:S(2)}) %collective-permute-start) | collective-permute-done | bytes 20512 | tf_op jit(solution)/shard_map/ppermute | solution.py:70
  89.4 0.1 fusion.11
  89.5 1.5 %collective-permute-start.1 = (f32[4,4,320]{2,1,0:T(4,128)S(1)}, f32[4,4,320]{2,1,0:T(4,128)S(1)}, u32[]{:S(2)}, u32[]{:S(2)}) collective-permute-start(f32[4,4,320]{2,1,0:T(4,128)S(1)} %fusion.11), channel_id=1, source_target_pairs={{0,2},{1,3},{2,0},{3,1},{4,6},{5,7},{6,4},{7,5},{8,10},{9,11},{10,... | collective-permute-start | bytes 61448 | tf_op jit(solution)/shard_map/ppermute | solution.py:70
  91.0 0.4 convolution_multiply_fusion
  91.4 1.0 %copy.26 = bf16[128,2048]{1,0:T(8,128)(2,1)} copy(bf16[128,2048]{0,1:T(8,128)(2,1)S(1)} %bitcast.47) | data formatting | bytes 1048576
  92.4 1.6 %copy.27 = f32[128,3072]{1,0:T(8,128)} copy(f32[128,3072]{0,1:T(8,128)S(1)} %bitcast.46) | data formatting | bytes 3145728
  94.0 0.0 collective-permute-done.1
  94.0 0.1 fusion.25
  94.1 0.1 slice_bitcast_fusion
  94.2 0.7 reshape.112
  94.9 0.6 copy.32
  (8 shorter events, 0.1 us)
Async XLA Ops:
  0.6 23.1 %copy-start = (bf16[4,768]{1,0:T(4,128)(2,1)S(1)}, bf16[4,768]{1,0:T(4,128)(2,1)}, u32[]{:S(2)}) copy-start(bf16[4,768]{1,0:T(4,128)(2,1)} %param.6) | copy-start | bytes 18436
  0.6 50.7 %copy-start.1 = (bf16[128,3072]{1,0:T(8,128)(2,1)S(1)}, bf16[128,3072]{1,0:T(8,128)(2,1)}, u32[]{:S(2)}) copy-start(bf16[128,3072]{1,0:T(8,128)(2,1)} %param.5) | copy-start | bytes 2359300
  0.7 51.0 %copy-start.2 = (s32[128]{0:T(128)S(1)}, s32[128]{0:T(128)}, u32[]{:S(2)}) copy-start(s32[128]{0:T(128)} %param.9) | copy-start | bytes 1540
  52.8 34.0 %copy-start.3 = (u32[32]{0:T(128)S(1)}, u32[32]{0:T(128)}, u32[]{:S(2)}) copy-start(u32[32]{0:T(128)} %constant.50) | copy-start | bytes 388
  88.2 1.2 %collective-permute-start = (f32[4,4,320]{2,1,0:T(4,128)S(1)}, f32[4,4,320]{2,1,0:T(4,128)S(1)}, u32[]{:S(2)}, u32[]{:S(2)}) collective-permute-start(f32[4,4,320]{2,1,0:T(4,128)S(1)} %broadcast_multiply_fusion), channel_id=1, source_target_pairs={{0,1},{1,0},{2,3},{3,2},{4,5},{5,4},{6,7},{7,6},{8,9},{9,8},{10,11... | collective-permute-start | bytes 61448 | tf_op jit(solution)/shard_map/ppermute | solution.py:70
  89.5 4.5 %collective-permute-start.1 = (f32[4,4,320]{2,1,0:T(4,128)S(1)}, f32[4,4,320]{2,1,0:T(4,128)S(1)}, u32[]{:S(2)}, u32[]{:S(2)}) collective-permute-start(f32[4,4,320]{2,1,0:T(4,128)S(1)} %fusion.11), channel_id=1, source_target_pairs={{0,2},{1,3},{2,0},{3,1},{4,6},{5,7},{6,4},{7,5},{8,10},{9,11},{10,... | collective-permute-start | bytes 61448 | tf_op jit(solution)/shard_map/ppermute | solution.py:70
